TPU v7x, 32 devices: a whole 2x2x4 slice. The times are simulated.
32 devices in a mesh: dp: 8 (over y, x, core), fsdp: 4 (over z).
Axes of the slice: x: 2, y: 2, z: 4, core: 2. Of those that a mesh axis runs over, the one named last changes fastest.
Arguments:
- activations: bfloat16 [8192, 4096], P(('dp', 'fsdp')), may hold values from -8 to 8
- cotangents: bfloat16 [8192, 4096], P('dp', 'fsdp'), may hold values from -8 to 8
- group_ids: int32 [32, 256], P(('dp', 'fsdp')), may hold values from 0 to 7, as said below
- weights: float32 [4096, 4096], P('fsdp', 'dp'), may hold values from -0.09375 to 0.09375
- first_moment: float32 [4096, 4096], P('fsdp', 'dp'), may hold values from -3 to 3
- second_moment: float32 [4096, 4096], P('fsdp', 'dp'), may hold values from 0.01 to 0.1
- fresh_noise: bfloat16 [4096, 4096], P('fsdp', 'dp'), may hold values from -6 to 6
- history: bfloat16 [16, 4096, 4096], P('dp', 'fsdp'), may hold values from -6 to 6
- slot_ids: int32 [16], P('dp'), may hold values from 0 to 15, each once
- band_coefs: float32 [16], replicated, may hold values from 0.3 to 1
- step_number: int32 [1], replicated, may hold values from 16 to 99999
- noise_mult: float32 [1], replicated, may hold values from 0.002 to 0.008
Outputs:
- new_weights: float32 [4096, 4096], P('fsdp', 'dp')
- new_first: float32 [4096, 4096], P('fsdp', 'dp')
- new_second: float32 [4096, 4096], P('fsdp', 'dp')
- noisy_mean: float32 [4096, 4096], P('fsdp', 'dp')
- gathered_weights: float32 [4096, 4096], P('fsdp')
- new_history: bfloat16 [16, 4096, 4096], P('dp', 'fsdp')
Inputs may be any that keep to these rules, and one draw needn't show every extreme that they name: `group_ids`: in each row the ids never fall; each of the 8 ids names 1 to 64 tokens, one of them exactly 64. `slot_ids`: each cycle position is held by exactly one entry.
All inputs are finite; a program needn't handle non-finite values.
Results may differ from a plain program's by a relative error of at most 0.002.
Values may be sent and summed in bfloat16 or wider, within the bound.
No kernel may reach another device: no remote copies, remote signals or barrier semaphores. Data moves between devices by JAX's collectives and lax.ppermute only.
A program may use at most 192 MiB of HBM per device.

v0:
```python
import jax
import jax.numpy as jnp
from jax import lax
from jax.sharding import PartitionSpec as P

D_IN = 4096
D_OUT = 4096
BAND = 16
GROUP_MOST = 64
EX_DEV = 8


def clip_bound():
    return ((GROUP_MOST * GROUP_MOST / 4.0 + GROUP_MOST) * D_IN * D_OUT) ** 0.5


def body(
    activations,
    cotangents,
    group_ids,
    weights,
    first_moment,
    second_moment,
    fresh_noise,
    history,
    slot_ids,
    band_coefs,
    step_number,
    noise_mult,
):
    clip = clip_bound()
    token_count = activations.shape[0]
    out_local = cotangents.shape[1]
    step_value = step_number[0]
    target = step_value % BAND
    full_fresh = lax.all_gather(fresh_noise, "dp", axis=1, tiled=True)
    new_history = jnp.where((slot_ids == target)[:, None, None], full_fresh[None], history)
    blocks = cotangents.reshape(cotangents.shape[0] // token_count, token_count, out_local)
    partial_gram = jnp.einsum("ati,asi->ats", blocks, blocks, preferred_element_type=jnp.float32)
    cotan_gram = lax.psum_scatter(partial_gram, "fsdp", scatter_dimension=0, tiled=True)[0]
    input_gram = lax.dot_general(
        activations, activations, (((1,), (1,)), ((), ())), preferred_element_type=jnp.float32
    )
    labels = group_ids[0]
    same = labels[:, None] == labels[None, :]
    row_terms = jnp.sum(jnp.where(same, input_gram * cotan_gram, 0.0), axis=1)
    squared = jnp.sum(jnp.where(same, row_terms[None, :], 0.0), axis=1)
    factor = clip / jnp.maximum(jnp.sqrt(squared), clip)
    scaled = (activations.astype(jnp.float32) * factor[:, None]).astype(jnp.bfloat16)
    gradient = lax.dot_general(
        cotangents,
        lax.all_gather(scaled, "fsdp", axis=0, tiled=True),
        (((0,), (0,)), ((), ())),
        preferred_element_type=jnp.float32,
    )
    lags = (step_value - slot_ids - 1) % BAND + 1
    columns = jnp.arange(BAND, dtype=jnp.int32)
    lag_weight = jnp.sum(
        jnp.where(columns[None, :] == lags[:, None], band_coefs[None, :], 0.0), axis=1
    )
    history_part = jnp.zeros(history.shape[1:], jnp.float32)
    for position in range(history.shape[0]):
        history_part = history_part + lag_weight[position] * history[position].astype(jnp.float32)
    noise_scale = noise_mult[0] * clip
    combined = lax.psum_scatter(
        gradient + noise_scale * history_part, "dp", scatter_dimension=1, tiled=True
    )
    examples = EX_DEV * lax.axis_size("dp") * lax.axis_size("fsdp")
    noisy_mean = (
        combined + noise_scale * band_coefs[0] * fresh_noise.astype(jnp.float32)
    ) / examples
    new_first = 0.9 * first_moment + 0.1 * noisy_mean
    new_second = 0.999 * second_moment + 0.001 * noisy_mean * noisy_mean
    step_float = step_value.astype(jnp.float32)
    corrected_first = new_first / (1.0 - jnp.power(jnp.float32(0.9), step_float))
    corrected_second = new_second / (1.0 - jnp.power(jnp.float32(0.999), step_float))
    new_weights = weights - 0.002 * corrected_first / (jnp.sqrt(corrected_second) + 1e-08)
    gathered_weights = lax.all_gather(new_weights, "dp", axis=1, tiled=True)
    return (new_weights, new_first, new_second, noisy_mean, gathered_weights, new_history)


def solution(mesh):
    in_specs = (
        P(("dp", "fsdp"), None),
        P("dp", "fsdp"),
        P(("dp", "fsdp"), None),
        P("fsdp", "dp"),
        P("fsdp", "dp"),
        P("fsdp", "dp"),
        P("fsdp", "dp"),
        P("dp", "fsdp", None),
        P("dp"),
        P(),
        P(),
        P(),
    )
    out_specs = (
        P("fsdp", "dp"),
        P("fsdp", "dp"),
        P("fsdp", "dp"),
        P("fsdp", "dp"),
        P("fsdp", None),
        P("dp", "fsdp", None),
    )
    return jax.shard_map(body, mesh=mesh, in_specs=in_specs, out_specs=out_specs, check_vma=False)
```

profile of v0, /device:TPU:0, one launch (start us, length us, event | category | flops | bytes accessed | tf_op | source)
XLA Modules:
  0.0 505.7 jit_solution(12465230712963849113)
XLA Ops:
  7.2 0.0 copy-start
  7.2 0.0 reduce-scatter.3.cloned.1.call-start
  7.2 1.5 copy-done
  8.8 0.0 copy-start.7
  8.8 1.7 fusion.8
  10.5 0.0 reduce-scatter.3.cloned.1.call-update
  10.5 0.0 all-gather.4.cloned.1.call-start
  10.6 30.3 %reduce-scatter.3.cloned.1.call-done = f32[1,256,256]{2,1,0:T(8,128)} async-done(((f32[4,256,256]{2,1,0:T(8,128)}), f32[1,256,256]{2,1,0:T(8,128)}) %reduce-scatter.3.cloned.1.call-update) | async-done | bytes 262160 | tf_op jit(solution)/shard_map/reduce_scatter | solution.py:40
  40.9 0.0 copy-done.7
  40.9 0.0 copy-start.6
  40.9 3.2 fusion.1
  44.1 0.2 fusion.2
  44.3 0.0 copy-done.6
  44.3 1.9 multiply_convert_fusion
  46.2 0.0 all-gather.4.cloned.1.call-update
  46.2 0.0 reduce-scatter.5.cloned.1.call-start
  46.9 12.1 %fusion.6 = (bf16[1,1024,4096]{2,1,0:T(8,128)(2,1)}, bf16[1,1024,4096]{2,1,0:T(8,128)(2,1)}) fusion(bf16[2,1024,4096]{2,1,0:T(8,128)(2,1)} %param.19), kind=kLoop, calls=%fused_computation.22 | loop fusion | bytes 33554432 | tf_op jit(solution)/shard_map/slice | solution.py:63
  59.1 11.9 %copy.41 = bf16[1,1024,4096]{1,2,0:T(8,128)(2,1)} copy(bf16[1,1024,4096]{2,1,0:T(8,128)(2,1)} %get-tuple-element.22) | data formatting | bytes 16777216
  71.0 0.0 copy-start.9
  71.0 0.0 copy-start.8
  71.0 12.0 %copy.40 = bf16[1,1024,4096]{1,2,0:T(8,128)(2,1)} copy(bf16[1,1024,4096]{2,1,0:T(8,128)(2,1)} %get-tuple-element.21) | data formatting | bytes 16777216
  83.6 0.0 copy-done.9
  83.7 0.0 copy-done.8
  83.7 0.2 fusion.3
  83.9 0.6 fusion.7
  84.5 110.1 %all-gather.4.cloned.1.call-done = bf16[1024,4096]{1,0:T(8,128)(2,1)} async-done(((bf16[256,4096]{1,0:T(8,128)(2,1)}), bf16[1024,4096]{1,0:T(8,128)(2,1)}) %all-gather.4.cloned.1.call-update) | async-done | bytes 8388624 | tf_op jit(solution)/shard_map/all_gather | solution.py:52
  194.5 22.8 %bitcast_add_fusion = f32[1024,4096]{0,1:T(8,128)} fusion(bf16[1,1024,4096]{1,2,0:T(8,128)(2,1)} %copy.41, bf16[1,1024,4096]{1,2,0:T(8,128)(2,1)} %copy.40, bf16[1024,4096]{1,0:T(8,128)(2,1)} %all-gather.4.cloned.1.call-done, bf16[1024,1024]{1,0:T(8,128)(2,1)S(1)} %copy-done, f32[]{:T(128)} %bitcast.7, f32[]{:T(128)} %bitcast.6, f32[]{:T(128)} %bitcast.4), kind=kOutput, calls=%fused_computation | convolution fusion | flops 8619294720 | bytes 44040204 | tf_op jit(solution)/shard_map/dot_general | solution.py:50
  217.3 0.0 copy-start.4
  217.3 0.0 reduce-scatter.5.cloned.1.call-update
  217.3 0.0 all-gather.8.cloned.1.call-start
  217.4 0.5 all-gather.8.cloned.1.call-update
  217.9 0.2 all-gather.6.cloned.1.call-start
  218.1 0.4 copy-done.4
  218.5 1.3 copy.32
  219.8 2.3 copy.34
  222.2 3.1 copy.29
  225.3 0.0 copy-start.5
  225.3 3.3 copy.33
  228.6 103.2 %reduce-scatter.5.cloned.1.call-done = f32[1024,512]{0,1:T(8,128)} async-done(((f32[1024,4096]{0,1:T(8,128)}), f32[1024,512]{0,1:T(8,128)}) %reduce-scatter.5.cloned.1.call-update) | async-done | bytes 2097168 | tf_op jit(solution)/shard_map/reduce_scatter | solution.py:65
  331.9 0.0 copy-done.5
  331.9 7.7 %divide_subtract_fusion = (f32[1024,512]{0,1:T(8,128)}, f32[1024,512]{0,1:T(8,128)}, f32[1024,512]{0,1:T(8,128)}, f32[1024,512]{0,1:T(8,128)}) fusion(f32[1024,512]{0,1:T(8,128)S(1)} %copy.34, f32[]{:T(128)S(6)} %sub.22, f32[]{:T(128)S(6)} %sub.21, f32[1024,512]{0,1:T(8,128)} %reduce-scatter.5.cloned.1.call-done, bf16[1024,512]{0,1:T(8,128)(2,1)S(1)} %copy-done.5, ...), kind=kLoop, calls=%fused_computation.3 | loop fusion | flops 8912896 | bytes 17825804 | tf_op jit(solution)/shard_map/sub | solution.py:77
  339.6 0.0 all-gather.6.cloned.1.call-update
  339.6 0.0 copy-start.2
  339.6 49.8 %all-gather.8.cloned.1.call-done = bf16[1024,4096]{1,0:T(8,128)(2,1)} async-done(((bf16[1024,512]{1,0:T(8,128)(2,1)}), bf16[1024,4096]{1,0:T(8,128)(2,1)}) %all-gather.8.cloned.1.call-update) | async-done | bytes 8388624 | tf_op jit(solution)/shard_map/all_gather | solution.py:36
  389.5 16.7 %broadcast_select_fusion = bf16[2,1024,4096]{2,1,0:T(8,128)(2,1)} fusion(bf16[2,1024,4096]{2,1,0:T(8,128)(2,1)} %param.19, pred[2]{0:T(512)(128)(4,1)S(1)} %broadcast_compare_fusion, bf16[1024,4096]{1,0:T(8,128)(2,1)} %all-gather.8.cloned.1.call-done), kind=kLoop, calls=%fused_computation.1 | loop fusion | flops 8388608 | bytes 41943040 | tf_op jit(solution)/shard_map/jit(_where)/select_n | solution.py:37
  406.2 0.0 copy-done.2
  406.2 1.8 copy.35
  408.0 2.9 copy.36
  410.9 0.0 copy-start.3
  410.9 3.0 copy.37
  413.9 0.0 copy-done.3
  413.9 1.8 copy.38
  415.7 65.8 %all-gather.6.cloned.1.call-done = f32[1024,4096]{0,1:T(8,128)} async-done(((f32[1024,512]{0,1:T(8,128)}), f32[1024,4096]{0,1:T(8,128)}) %all-gather.6.cloned.1.call-update) | async-done | bytes 16777232 | tf_op jit(solution)/shard_map/all_gather | solution.py:78
  481.6 0.0 copy-start.1
  481.6 17.6 %copy.39 = f32[1024,4096]{1,0:T(8,128)} copy(f32[1024,4096]{0,1:T(8,128)} %all-gather.6.cloned.1.call-done) | data formatting | bytes 33554432
  499.1 0.0 copy-done.1
  (3 shorter events, 0.0 us)
Async XLA Ops:
  7.2 1.6 copy-start
  7.2 33.7 %reduce-scatter.3.cloned.1.call-start = ((), (), s32[]{:S(2)}) async-start(), calls=%async_computation.2 | async-start | bytes 1310720 | tf_op jit(solution)/shard_map/reduce_scatter | solution.py:40
  8.8 32.1 %copy-start.7 = (s32[1,256]{1,0:T(1,128)S(1)}, s32[1,256]{1,0:T(1,128)}, u32[]{:S(2)}) copy-start(s32[1,256]{1,0:T(1,128)} %param.14) | copy-start | bytes 3076
  10.5 184.0 %all-gather.4.cloned.1.call-start = ((), (), s32[]{:S(2)}) async-start(), calls=%async_computation.3 | async-start | bytes 10485760 | tf_op jit(solution)/shard_map/all_gather | solution.py:52
  40.9 3.4 copy-start.6
  46.2 285.6 %reduce-scatter.5.cloned.1.call-start = ((), (), s32[]{:S(2)}) async-start(), calls=%async_computation.4 | async-start | bytes 18874368 | tf_op jit(solution)/shard_map/reduce_scatter | solution.py:65
  71.0 12.6 %copy-start.9 = (s32[2]{0:T(128)S(1)}, s32[2]{0:T(128)}, u32[]{:S(2)}) copy-start(s32[2]{0:T(128)} %param.20) | copy-start | bytes 28
  71.0 12.7 %copy-start.8 = (f32[16]{0:T(128)S(1)}, f32[16]{0:T(128)}, u32[]{:S(2)}) copy-start(f32[16]{0:T(128)} %param.21) | copy-start | bytes 196
  217.3 1.2 copy-start.4
  217.3 172.2 %all-gather.8.cloned.1.call-start = ((), (), s32[]{:S(2)}) async-start(), calls=%async_computation.6 | async-start | bytes 9437184 | tf_op jit(solution)/shard_map/all_gather | solution.py:36
  217.9 263.7 %all-gather.6.cloned.1.call-start = ((), (), s32[]{:S(2)}) async-start(), calls=%async_computation.5 | async-start | bytes 18874368 | tf_op jit(solution)/shard_map/all_gather | solution.py:78
  225.3 106.6 %copy-start.5 = (bf16[1024,512]{0,1:T(8,128)(2,1)S(1)}, bf16[1024,512]{0,1:T(8,128)(2,1)}, u32[]{:S(2)}) copy-start(bf16[1024,512]{0,1:T(8,128)(2,1)} %copy.32) | copy-start | bytes 3145732
  339.6 66.6 %copy-start.2 = (f32[1024,512]{0,1:T(8,128)S(1)}, f32[1024,512]{0,1:T(8,128)}, u32[]{:S(2)}) copy-start(f32[1024,512]{0,1:T(8,128)} %get-tuple-element.18) | copy-start | bytes 6291460
  410.9 3.0 copy-start.3
  481.6 17.6 %copy-start.1 = (bf16[1024,1024]{1,0:T(8,128)(2,1)S(1)}, bf16[1024,1024]{1,0:T(8,128)(2,1)}, u32[]{:S(2)}) copy-start(bf16[1024,1024]{1,0:T(8,128)(2,1)} %param.13) | copy-start | bytes 6291460
Sparse Core Ops, SparseCore 0:
  10.9 29.9 reduce-scatter.2
  46.4 148.1 all-gather.3
  217.4 114.3 reduce-scatter.4
  333.6 55.8 all-gather.7
  391.8 89.7 all-gather.5
where the time goes:
time: 507 us; the launch traced here: 506 us
  waiting for transfers between devices  360 us (71%)
  local copies, waits for them, and re-layouts  75.7 us (15%)
  matrix products  27.7 us (5%)
  other arithmetic  26.8 us (5%)
  between operations  15.3 us (3%)
    all_gather x1, waiting for transfers between devices, body(): lax.all_gather(scaled, 'fsdp', axis=0, tiled=True)  110 us
    reduce_scatter x1, waiting for transfers between devices, body(): lax.psum_scatter(gradient + noise_scale * history_part, 'dp', scatter_dim...  103 us
    all_gather x1, waiting for transfers between devices, body(): gathered_weights = lax.all_gather(new_weights, 'dp', axis=1, tiled=True)  65.8 us
    unnamed x31, local copies, waits for them, and re-layouts  62.9 us
    all_gather x1, waiting for transfers between devices, body(): full_fresh = lax.all_gather(fresh_noise, 'dp', axis=1, tiled=True)  49.8 us
    reduce_scatter x1, waiting for transfers between devices, body(): lax.psum_scatter(partial_gram, 'fsdp', scatter_dimension=0, tiled=True)[0]  30.3 us
    dot_general x1, matrix products, body(): lax.dot_general(cotangents, lax.all_gather(scaled, 'fsdp', axis=0, tiled=...  22.8 us
    select_n x1, other arithmetic, body(): jnp.where((slot_ids == target)[:, None, None], full_fresh[None], history)  16.7 us
  transfers between devices with their start and end apart: 5, of which 5 were waited for; matrix products, arithmetic and copies ran while one was open for 16% of the time, Pallas kernels for 0%

commit v1 on v0

--- a/solution.py
+++ b/solution.py
@@ -8,6 +8,19 @@
 BAND = 16
 GROUP_MOST = 64
 EX_DEV = 8
+
+
+def collect(x, axis, dim):
+    ways = lax.axis_size(axis)
+    up = [(d, (d + 1) % ways) for d in range(ways)]
+    down = [(d, (d - 1) % ways) for d in range(ways)]
+    earlier, later = ([x], [x])
+    for _ in range(ways // 2):
+        earlier.append(lax.ppermute(earlier[-1], axis, up))
+    for _ in range((ways - 1) // 2):
+        later.append(lax.ppermute(later[-1], axis, down))
+    line = jnp.concatenate([*earlier[::-1], *later[1:]], axis=dim)
+    return jnp.roll(line, (lax.axis_index(axis) - ways // 2) * x.shape[dim], axis=dim)
 
 
 def clip_bound():
@@ -75,7 +88,7 @@
     corrected_first = new_first / (1.0 - jnp.power(jnp.float32(0.9), step_float))
     corrected_second = new_second / (1.0 - jnp.power(jnp.float32(0.999), step_float))
     new_weights = weights - 0.002 * corrected_first / (jnp.sqrt(corrected_second) + 1e-08)
-    gathered_weights = lax.all_gather(new_weights, "dp", axis=1, tiled=True)
+    gathered_weights = collect(new_weights, "dp", 1)
     return (new_weights, new_first, new_second, noisy_mean, gathered_weights, new_history)
 
 

time: 507 us -> 594 us (1.17)
  waiting for transfers between devices: 360 us -> 413 us
  local copies, waits for them, and re-layouts: 75.7 us -> 103 us
  starting transfers between devices: 0.38 us -> 8.32 us
    ppermute x0 -> x7, waiting for transfers between devices: none -> 167 us  [the longest x4 167 us: collect(): earlier.append(lax.ppermute(earlier[-1], axis, up))]
    all_gather x1 -> x0, waiting for transfers between devices: 65.8 us -> none  [body(): gathered_weights = lax.all_gather(new_weights, 'dp', axis=1, tiled=True)]
    all_gather x1, waiting for transfers between devices: 49.8 us -> 0.01 us  [body(): full_fresh = lax.all_gather(fresh_noise, 'dp', axis=1, tiled=True)]
    unnamed x31 -> x50, local copies, waits for them, and re-layouts: 62.9 us -> 82.1 us
    ppermute x0 -> x7, starting transfers between devices: none -> 7.97 us  [the longest x3 7.41 us: collect(): later.append(lax.ppermute(later[-1], axis, down))]
    dynamic_slice x0 -> x1, local copies, waits for them, and re-layouts: none -> 6.08 us  [collect(): jnp.roll(line, (lax.axis_index(axis) - ways // 2) * x.shape[dim], axis=dim)]
  transfers between devices with their start and end apart: 5 -> 11, of which waited for: 5 -> 7; matrix products, arithmetic and copies ran while one was open for 16% -> 15% of each run, Pallas kernels for 0% -> 0%
where the time goes in v1:
time: 594 us; the launch traced here: 593 us
  waiting for transfers between devices  413 us (70%)
  local copies, waits for them, and re-layouts  103 us (17%)
  matrix products  27.7 us (5%)
  other arithmetic  25.6 us (4%)
  between operations  15.4 us (3%)
  starting transfers between devices  8.32 us (1%)
    ppermute x4, waiting for transfers between devices, collect(): earlier.append(lax.ppermute(earlier[-1], axis, up))  167 us
    all_gather x1, waiting for transfers between devices, body(): lax.all_gather(scaled, 'fsdp', axis=0, tiled=True)  110 us
    reduce_scatter x1, waiting for transfers between devices, body(): lax.psum_scatter(gradient + noise_scale * history_part, 'dp', scatter_dim...  105 us
    unnamed x50, local copies, waits for them, and re-layouts  82.1 us
    reduce_scatter x1, waiting for transfers between devices, body(): lax.psum_scatter(partial_gram, 'fsdp', scatter_dimension=0, tiled=True)[0]  30.4 us
    dot_general x1, matrix products, body(): lax.dot_general(cotangents, lax.all_gather(scaled, 'fsdp', axis=0, tiled=...  22.8 us
    select_n x1, other arithmetic, body(): jnp.where((slot_ids == target)[:, None, None], full_fresh[None], history)  15.6 us
    slice x1, local copies, waits for them, and re-layouts, body(): history[position].astype(jnp.float32)  12.1 us
  transfers between devices with their start and end apart: 11, of which 7 were waited for; matrix products, arithmetic and copies ran while one was open for 15% of the time, Pallas kernels for 0%

profile of v1, /device:TPU:0, one launch (start us, length us, event | category | flops | bytes accessed | tf_op | source)
XLA Modules:
  0.0 593.1 jit_solution(18271576591954307659)
XLA Ops:
  7.2 0.0 copy-start
  7.2 0.0 reduce-scatter.3.cloned.1.call-start
  7.2 1.5 copy-done
  8.8 1.7 fusion.8
  10.5 0.0 reduce-scatter.3.cloned.1.call-update
  10.5 0.0 all-gather.3.cloned.1.call-start
  10.6 30.4 %reduce-scatter.3.cloned.1.call-done = f32[1,256,256]{2,1,0:T(8,128)} async-done(((f32[4,256,256]{2,1,0:T(8,128)}), f32[1,256,256]{2,1,0:T(8,128)}) %reduce-scatter.3.cloned.1.call-update) | async-done | bytes 262160 | tf_op jit(solution)/shard_map/reduce_scatter | solution.py:53
  40.9 3.2 fusion.1
  44.1 0.2 fusion.2
  44.3 1.9 multiply_convert_fusion
  46.2 0.0 all-gather.3.cloned.1.call-update
  46.3 0.0 reduce-scatter.5.cloned.1.call-start
  47.0 12.1 %fusion.6 = (bf16[1,1024,4096]{2,1,0:T(8,128)(2,1)}, bf16[1,1024,4096]{2,1,0:T(8,128)(2,1)}) fusion(bf16[2,1024,4096]{2,1,0:T(8,128)(2,1)} %param.19), kind=kLoop, calls=%fused_computation.39 | loop fusion | bytes 33554432 | tf_op jit(solution)/shard_map/slice | solution.py:76
  59.1 12.0 %copy.40 = bf16[1,1024,4096]{1,2,0:T(8,128)(2,1)} copy(bf16[1,1024,4096]{2,1,0:T(8,128)(2,1)} %get-tuple-element.21) | data formatting | bytes 16777216
  71.1 12.0 %copy.41 = bf16[1,1024,4096]{1,2,0:T(8,128)(2,1)} copy(bf16[1,1024,4096]{2,1,0:T(8,128)(2,1)} %get-tuple-element.22) | data formatting | bytes 16777216
  83.8 0.2 fusion.3
  83.9 0.6 fusion.7
  84.5 110.0 %all-gather.3.cloned.1.call-done = bf16[1024,4096]{1,0:T(8,128)(2,1)} async-done(((bf16[256,4096]{1,0:T(8,128)(2,1)}), bf16[1024,4096]{1,0:T(8,128)(2,1)}) %all-gather.3.cloned.1.call-update) | async-done | bytes 8388624 | tf_op jit(solution)/shard_map/all_gather | solution.py:65
  194.5 22.8 %bitcast_add_fusion = f32[1024,4096]{0,1:T(8,128)} fusion(bf16[1,1024,4096]{1,2,0:T(8,128)(2,1)} %copy.41, bf16[1,1024,4096]{1,2,0:T(8,128)(2,1)} %copy.40, bf16[1024,4096]{1,0:T(8,128)(2,1)} %all-gather.3.cloned.1.call-done, bf16[1024,1024]{1,0:T(8,128)(2,1)S(1)} %copy-done, f32[]{:T(128)} %bitcast.7, f32[]{:T(128)} %bitcast.6, f32[]{:T(128)} %bitcast.4), kind=kOutput, calls=%fused_computation | convolution fusion | flops 8619294720 | bytes 44040204 | tf_op jit(solution)/shard_map/dot_general | solution.py:63
  217.3 0.0 reduce-scatter.5.cloned.1.call-update
  217.3 0.0 copy-start.7
  217.3 0.2 all-gather.5.cloned.1.call-start
  217.6 0.3 all-gather.5.cloned.1.call-update
  217.9 0.6 copy-done.4
  218.5 1.3 copy.32
  220.0 1.8 copy.29
  221.8 3.0 copy.33
  224.8 1.8 copy.34
  226.6 105.2 %reduce-scatter.5.cloned.1.call-done = f32[1024,512]{0,1:T(8,128)} async-done(((f32[1024,4096]{0,1:T(8,128)}), f32[1024,512]{0,1:T(8,128)}) %reduce-scatter.5.cloned.1.call-update) | async-done | bytes 2097168 | tf_op jit(solution)/shard_map/reduce_scatter | solution.py:78
  331.9 7.6 %divide_subtract_fusion = (f32[1024,512]{0,1:T(8,128)S(1)}, f32[1024,512]{0,1:T(8,128)}, f32[1024,512]{0,1:T(8,128)}, f32[1024,512]{0,1:T(8,128)}) fusion(f32[1024,512]{0,1:T(8,128)} %copy.34, f32[]{:T(128)S(6)} %sub.29, f32[]{:T(128)S(6)} %sub.28, f32[1024,512]{0,1:T(8,128)} %reduce-scatter.5.cloned.1.call-done, bf16[1024,512]{0,1:T(8,128)(2,1)S(1)} %copy-done.5, ...), kind=kLoop, calls=%fused_computation.3 | loop fusion | flops 8912896 | bytes 17825804 | tf_op jit(solution)/shard_map/sub | solution.py:90
  339.5 0.0 collective-permute-start
  339.5 52.6 %collective-permute-done = f32[1024,512]{0,1:T(8,128)S(1)} collective-permute-done((f32[1024,512]{0,1:T(8,128)S(1)}, f32[1024,512]{0,1:T(8,128)S(1)}, u32[]{:S(2)}, u32[]{:S(2)}) %collective-permute-start) | collective-permute-done | bytes 2097184 | tf_op jit(solution)/shard_map/ppermute | solution.py:19
  392.2 0.6 collective-permute-start.1
  392.7 2.1 collective-permute-start.4
  394.8 49.8 %collective-permute-done.1 = f32[1024,512]{0,1:T(8,128)} collective-permute-done((f32[1024,512]{0,1:T(8,128)S(1)}, f32[1024,512]{0,1:T(8,128)}, u32[]{:S(2)}, u32[]{:S(2)}) %collective-permute-start.1) | collective-permute-done | bytes 2097184 | tf_op jit(solution)/shard_map/ppermute | solution.py:19
  444.6 0.0 collective-permute-start.2
  444.6 0.0 collective-permute-done.4
  444.6 2.6 collective-permute-start.5
  447.3 45.9 %collective-permute-done.2 = f32[1024,512]{0,1:T(8,128)} collective-permute-done((f32[1024,512]{0,1:T(8,128)}, f32[1024,512]{0,1:T(8,128)}, u32[]{:S(2)}, u32[]{:S(2)}) %collective-permute-start.2) | collective-permute-done | bytes 2097184 | tf_op jit(solution)/shard_map/ppermute | solution.py:19
  493.2 2.7 collective-permute-start.6
  495.9 15.6 %broadcast_select_fusion = bf16[2,1024,4096]{2,1,0:T(8,128)(2,1)} fusion(bf16[2,1024,4096]{2,1,0:T(8,128)(2,1)} %param.19, pred[2]{0:T(512)(128)(4,1)S(1)} %broadcast_compare_fusion, bf16[1024,4096]{1,0:T(8,128)(2,1)} %all-gather.5.cloned.1.call-done), kind=kLoop, calls=%fused_computation.1 | loop fusion | flops 8388608 | bytes 41943040 | tf_op jit(solution)/shard_map/jit(_where)/select_n | solution.py:50
  511.5 1.8 copy.35
  513.3 2.9 copy.36
  516.2 2.9 copy.37
  519.1 2.9 copy.38
  521.9 19.1 %collective-permute-done.3 = f32[1024,512]{0,1:T(8,128)} collective-permute-done((f32[1024,512]{0,1:T(8,128)}, f32[1024,512]{0,1:T(8,128)}, u32[]{:S(2)}, u32[]{:S(2)}) %collective-permute-start.3) | collective-permute-done | bytes 2097184 | tf_op jit(solution)/shard_map/ppermute | solution.py:19
  541.1 1.7 constant_dynamic-update-slice_fusion.15
  542.8 1.9 constant_dynamic-update-slice_fusion.14
  544.7 1.7 constant_dynamic-update-slice_fusion.13
  546.5 0.2 constant_dynamic-update-slice_fusion.12
  546.7 0.1 constant_dynamic-update-slice_fusion.11
  546.9 1.7 constant_dynamic-update-slice_fusion.10
  548.6 1.7 constant_dynamic-update-slice_fusion.9
  550.3 1.7 constant_dynamic-update-slice_fusion.8
  552.1 1.7 constant_dynamic-update-slice_fusion.7
  553.8 1.7 constant_dynamic-update-slice_fusion.6
  555.5 1.7 constant_dynamic-update-slice_fusion.5
  557.3 0.2 constant_dynamic-update-slice_fusion.4
  557.5 0.1 constant_dynamic-update-slice_fusion.3
  557.7 1.7 constant_dynamic-update-slice_fusion.2
  559.4 1.7 constant_dynamic-update-slice_fusion.1
  561.1 1.7 constant_dynamic-update-slice_fusion
  562.9 6.1 %constant_dynamic-slice_fusion = f32[1024,4096]{0,1:T(8,128)} fusion(f32[1024,8192]{0,1:T(8,128)S(1)} %constant_dynamic-update-slice_fusion, s32[]{:T(128)S(6)} %select_n.46), kind=kLoop, calls=%fused_computation.38 | loop fusion | bytes 33554436 | tf_op jit(solution)/shard_map/jit(_roll_dynamic)/dynamic_slice | solution.py:23
  569.0 17.6 %copy.39 = f32[1024,4096]{1,0:T(8,128)} copy(f32[1024,4096]{0,1:T(8,128)} %constant_dynamic-slice_fusion) | data formatting | bytes 33554432
  (27 shorter events, 0.1 us)
Async XLA Ops:
  7.2 1.6 copy-start
  7.2 33.7 %copy-start.9 = (s32[1,256]{1,0:T(1,128)S(1)}, s32[1,256]{1,0:T(1,128)}, u32[]{:S(2)}) copy-start(s32[1,256]{1,0:T(1,128)} %param.14) | copy-start | bytes 3076
  7.2 33.7 %reduce-scatter.3.cloned.1.call-start = ((), (), s32[]{:S(2)}) async-start(), calls=%async_computation.2 | async-start | bytes 1310720 | tf_op jit(solution)/shard_map/reduce_scatter | solution.py:53
  10.5 184.0 %all-gather.3.cloned.1.call-start = ((), (), s32[]{:S(2)}) async-start(), calls=%async_computation.3 | async-start | bytes 10485760 | tf_op jit(solution)/shard_map/all_gather | solution.py:65
  40.9 3.4 copy-start.6
  46.3 285.6 %reduce-scatter.5.cloned.1.call-start = ((), (), s32[]{:S(2)}) async-start(), calls=%async_computation.4 | async-start | bytes 18874368 | tf_op jit(solution)/shard_map/reduce_scatter | solution.py:78
  71.1 12.6 %copy-start.11 = (s32[2]{0:T(128)S(1)}, s32[2]{0:T(128)}, u32[]{:S(2)}) copy-start(s32[2]{0:T(128)} %param.20) | copy-start | bytes 28
  71.1 12.7 %copy-start.10 = (f32[16]{0:T(128)S(1)}, f32[16]{0:T(128)}, u32[]{:S(2)}) copy-start(f32[16]{0:T(128)} %param.21) | copy-start | bytes 196
  217.3 1.2 copy-start.4
  217.3 2.6 copy-start.7
  217.3 278.5 %all-gather.5.cloned.1.call-start = ((), (), s32[]{:S(2)}) async-start(), calls=%async_computation.5 | async-start | bytes 9437184 | tf_op jit(solution)/shard_map/all_gather | solution.py:49
  221.8 3.0 copy-start.8
  221.8 110.1 %copy-start.5 = (bf16[1024,512]{0,1:T(8,128)(2,1)S(1)}, bf16[1024,512]{0,1:T(8,128)(2,1)}, u32[]{:S(2)}) copy-start(bf16[1024,512]{0,1:T(8,128)(2,1)} %copy.32) | copy-start | bytes 3145732
  339.5 52.6 %collective-permute-start = (f32[1024,512]{0,1:T(8,128)S(1)}, f32[1024,512]{0,1:T(8,128)S(1)}, u32[]{:S(2)}, u32[]{:S(2)}) collective-permute-start(f32[1024,512]{0,1:T(8,128)S(1)} %get-tuple-element.18), channel_id=1, source_target_pairs={{0,4},{4,8},{8,12},{12,16},{16,20},{20,24},{24,28},{28,0},{1,5},{5... | collective-permute-start | bytes 6291464 | tf_op jit(solution)/shard_map/ppermute | solution.py:19
  392.2 52.5 %copy-start.2 = (f32[1024,512]{0,1:T(8,128)}, f32[1024,512]{0,1:T(8,128)S(1)}, u32[]{:S(2)}) copy-start(f32[1024,512]{0,1:T(8,128)S(1)} %collective-permute-done) | copy-start | bytes 6291460
  392.2 52.5 %collective-permute-start.1 = (f32[1024,512]{0,1:T(8,128)S(1)}, f32[1024,512]{0,1:T(8,128)}, u32[]{:S(2)}, u32[]{:S(2)}) collective-permute-start(f32[1024,512]{0,1:T(8,128)S(1)} %collective-permute-done), channel_id=1, source_target_pairs={{0,4},{4,8},{8,12},{12,16},{16,20},{20,24},{24,28},{28,0},{1,5},{5... | collective-permute-start | bytes 6291464 | tf_op jit(solution)/shard_map/ppermute | solution.py:19
  392.7 51.9 %collective-permute-start.4 = (f32[1024,512]{0,1:T(8,128)S(1)}, f32[1024,512]{0,1:T(8,128)}, u32[]{:S(2)}, u32[]{:S(2)}) collective-permute-start(f32[1024,512]{0,1:T(8,128)S(1)} %get-tuple-element.18), channel_id=1, source_target_pairs={{0,28},{4,0},{8,4},{12,8},{16,12},{20,16},{24,20},{28,24},{1,29},{... | collective-permute-start | bytes 6291464 | tf_op jit(solution)/shard_map/ppermute | solution.py:21
  444.6 48.5 %collective-permute-start.2 = (f32[1024,512]{0,1:T(8,128)}, f32[1024,512]{0,1:T(8,128)}, u32[]{:S(2)}, u32[]{:S(2)}) collective-permute-start(f32[1024,512]{0,1:T(8,128)} %collective-permute-done.1), channel_id=1, source_target_pairs={{0,4},{4,8},{8,12},{12,16},{16,20},{20,24},{24,28},{28,0},{1,5},{5... | collective-permute-start | bytes 6291464 | tf_op jit(solution)/shard_map/ppermute | solution.py:19
  444.6 48.5 %collective-permute-start.5 = (f32[1024,512]{0,1:T(8,128)}, f32[1024,512]{0,1:T(8,128)}, u32[]{:S(2)}, u32[]{:S(2)}) collective-permute-start(f32[1024,512]{0,1:T(8,128)} %collective-permute-done.4), channel_id=1, source_target_pairs={{0,28},{4,0},{8,4},{12,8},{16,12},{20,16},{24,20},{28,24},{1,29},{... | collective-permute-start | bytes 6291464 | tf_op jit(solution)/shard_map/ppermute | solution.py:21
  493.2 47.9 %collective-permute-start.3 = (f32[1024,512]{0,1:T(8,128)}, f32[1024,512]{0,1:T(8,128)}, u32[]{:S(2)}, u32[]{:S(2)}) collective-permute-start(f32[1024,512]{0,1:T(8,128)} %collective-permute-done.2), channel_id=1, source_target_pairs={{0,4},{4,8},{8,12},{12,16},{16,20},{20,24},{24,28},{28,0},{1,5},{5... | collective-permute-start | bytes 6291464 | tf_op jit(solution)/shard_map/ppermute | solution.py:19
  493.2 57.1 %collective-permute-start.6 = (f32[1024,512]{0,1:T(8,128)}, f32[1024,512]{0,1:T(8,128)}, u32[]{:S(2)}, u32[]{:S(2)}) collective-permute-start(f32[1024,512]{0,1:T(8,128)} %collective-permute-done.5), channel_id=1, source_target_pairs={{0,28},{4,0},{8,4},{12,8},{16,12},{20,16},{24,20},{28,24},{1,29},{... | collective-permute-start | bytes 6291464 | tf_op jit(solution)/shard_map/ppermute | solution.py:21
  542.8 3.6 copy-start.3
  568.9 17.6 %copy-start.1 = (bf16[1024,1024]{1,0:T(8,128)(2,1)S(1)}, bf16[1024,1024]{1,0:T(8,128)(2,1)}, u32[]{:S(2)}) copy-start(bf16[1024,1024]{1,0:T(8,128)(2,1)} %param.13) | copy-start | bytes 6291460
Sparse Core Ops, SparseCore 0:
  10.9 29.9 reduce-scatter.2
  46.4 148.1 all-gather.2
  217.4 114.3 reduce-scatter.4
  333.6 70.7 all-gather.4
